TPU v7x, 32 devices: a whole 2x2x4 slice. The times are simulated.
32 devices in a mesh: blk: 8 (over z, core), vb: 4 (over y, x).
Axes of the slice: x: 2, y: 2, z: 4, core: 2. Of those that a mesh axis runs over, the one named last changes fastest.
Arguments:
- amplitudes: float32 [32, 1024, 1024], P('blk', 'vb'), may hold values from -6 to 6
- integrals: float32 [2048, 1024], P('blk'), may hold values from -0.5 to 0.5
- row_orbitals: int32 [2048], P('blk'), may hold values from 0 to 1023
- pair_orbitals: int32 [32, 2], P('blk'), may hold values from 0 to 255
- occupied_energy: float32 [256], replicated, may hold values from -2 to -0.5
- virtual_energy: float32 [1024], replicated, may hold values from 0.5 to 3
Outputs:
- density: float32 [32, 1024, 1024], P('blk', 'vb')
All inputs are finite; a program needn't handle non-finite values.
Results may differ from a plain program's by a relative error of at most 0.0003.
Values sent between devices are 32-bit elements; how exact they have to be, the bound alone decides.
No kernel may reach another device: no remote copies, remote signals or barrier semaphores. Data moves between devices by JAX's collectives and lax.ppermute only.
A program may use at most 64 MiB of HBM per device.

v0:
```python
import jax
import jax.numpy as jnp
from jax import lax
from jax.sharding import PartitionSpec as P

HOPS = 5


def passed_along(block, axis, distance):
    devices = range(lax.axis_size(axis))
    route = [((i - distance) % len(devices), i) for i in devices]
    return lax.ppermute(block, axis, route)


def step_down(carried):
    return passed_along(carried, "blk", 1)


def local(amplitudes, integrals, row_orbitals, pair_orbitals, occupied_energy, virtual_energy):
    width = virtual_energy.shape[0]
    nocc = occupied_energy.shape[0]
    quarter = width // lax.axis_size("vb")
    qstart = lax.axis_index("vb") * quarter
    virt_iota = jnp.arange(width, dtype=jnp.int32)
    occ_iota = jnp.arange(nocc, dtype=jnp.int32)
    row_energy = jnp.sum(
        jnp.where(row_orbitals[:, None] == virt_iota[None, :], virtual_energy[None, :], 0.0), axis=1
    )
    pair_match = pair_orbitals[:, :, None] == occ_iota[None, None, :]
    pair_energy = jnp.sum(jnp.where(pair_match, occupied_energy[None, None, :], 0.0), axis=(1, 2))
    own_virtual = lax.dynamic_slice_in_dim(virtual_energy, qstart, quarter, 0)
    own = (integrals, row_energy)
    window = [own]
    current = passed_along((own[0], own[1]), "blk", -(HOPS - HOPS // 2))
    window = [current]
    for turn in range(HOPS):
        current = step_down(current)
        window.append(current)
    factors = lax.all_to_all(amplitudes, "vb", split_axis=2, concat_axis=1, tiled=True)

    def pair_columns(inputs):
        factor, energy = inputs
        total = jnp.zeros((width, quarter), jnp.float32)
        for block, energies in window:
            denom = energies[:, None] + own_virtual[None, :] - energy
            weighted = jnp.dot(
                block, factor, precision=lax.Precision.HIGHEST, preferred_element_type=jnp.float32
            )
            total = total + jnp.dot(
                block.T,
                weighted / denom,
                precision=lax.Precision.HIGHEST,
                preferred_element_type=jnp.float32,
            )
        return total

    totals = lax.map(pair_columns, (factors, pair_energy))
    return lax.all_to_all(totals, "vb", split_axis=1, concat_axis=2, tiled=True)


def solution(mesh):
    return jax.shard_map(
        local,
        mesh=mesh,
        in_specs=(P("blk", "vb", None), P("blk", None), P("blk"), P("blk", None), P(), P()),
        out_specs=P("blk", "vb", None),
        check_vma=False,
    )
```

profile of v0, /device:TPU:0, one launch (start us, length us, event | category | flops | bytes accessed | tf_op | source)
XLA Modules:
  0.0 425.2 jit_solution(7205439664500854542)
XLA Ops:
  0.0 3.5 collective-permute-start
  3.5 22.9 %collective-permute-done = f32[256,1024]{1,0:T(8,128)S(1)} collective-permute-done((f32[256,1024]{1,0:T(8,128)}, f32[256,1024]{1,0:T(8,128)S(1)}, u32[]{:S(2)}, u32[]{:S(2)}) %collective-permute-start) | collective-permute-done | bytes 1048608 | tf_op jit(solution)/shard_map/ppermute | solution.py:12
  26.4 12.8 %collective-permute-start.2 = (f32[256,1024]{1,0:T(8,128)S(1)}, f32[256,1024]{1,0:T(8,128)S(1)}, u32[]{:S(2)}, u32[]{:S(2)}) collective-permute-start(f32[256,1024]{1,0:T(8,128)S(1)} %collective-permute-done), channel_id=1, source_target_pairs={{28,0},{0,4},{4,8},{8,12},{12,16},{16,20},{20,24},{24,28},{29,1},{... | collective-permute-start | bytes 3145736 | tf_op jit(solution)/shard_map/ppermute | solution.py:12
  39.2 15.6 %collective-permute-done.2 = f32[256,1024]{1,0:T(8,128)S(1)} collective-permute-done((f32[256,1024]{1,0:T(8,128)S(1)}, f32[256,1024]{1,0:T(8,128)S(1)}, u32[]{:S(2)}, u32[]{:S(2)}) %collective-permute-start.2) | collective-permute-done | bytes 1048608 | tf_op jit(solution)/shard_map/ppermute | solution.py:12
  54.8 5.3 %copy.15 = f32[4,256,1024]{1,0,2:T(4,128)} copy(f32[4,256,1024]{2,1,0:T(8,128)} %param.8) | data formatting | bytes 8388608 | tf_op args[0]
  60.1 5.0 %all-to-all-start = ((f32[4,256,1024]{1,0,2:T(4,128)}), f32[4,256,1024]{1,0,2:T(4,128)}, u32[]{:S(2)}, u32[]{:S(2)}) async-start(f32[4,256,1024]{1,0,2:T(4,128)} %copy.15), calls=%async_computation | async-start | bytes 8388608 | tf_op jit(solution)/shard_map/all_to_all | solution.py:39
  65.1 5.7 %collective-permute-done.4 = f32[256,1024]{1,0:T(8,128)S(1)} collective-permute-done((f32[256,1024]{1,0:T(8,128)S(1)}, f32[256,1024]{1,0:T(8,128)S(1)}, u32[]{:S(2)}, u32[]{:S(2)}) %collective-permute-start.4) | collective-permute-done | bytes 1048608 | tf_op jit(solution)/shard_map/ppermute | solution.py:12
  70.8 16.0 %collective-permute-done.6 = f32[256,1024]{1,0:T(8,128)S(1)} collective-permute-done((f32[256,1024]{1,0:T(8,128)S(1)}, f32[256,1024]{1,0:T(8,128)S(1)}, u32[]{:S(2)}, u32[]{:S(2)}) %collective-permute-start.6) | collective-permute-done | bytes 1048608 | tf_op jit(solution)/shard_map/ppermute | solution.py:12
  87.9 16.1 %collective-permute-done.8 = f32[256,1024]{1,0:T(8,128)} collective-permute-done((f32[256,1024]{1,0:T(8,128)S(1)}, f32[256,1024]{1,0:T(8,128)}, u32[]{:S(2)}, u32[]{:S(2)}) %collective-permute-start.8) | collective-permute-done | bytes 1048608 | tf_op jit(solution)/shard_map/ppermute | solution.py:12
  104.4 3.0 collective-permute-done.1
  107.4 3.0 collective-permute-start.3
  110.3 10.6 %collective-permute-done.3 = f32[256]{0:T(256)S(1)} collective-permute-done((f32[256]{0:T(256)S(1)}, f32[256]{0:T(256)S(1)}, u32[]{:S(2)}, u32[]{:S(2)}) %collective-permute-start.3) | collective-permute-done | bytes 1056 | tf_op jit(solution)/shard_map/ppermute | solution.py:12
  120.9 4.8 %collective-permute-done.5 = f32[256]{0:T(256)S(1)} collective-permute-done((f32[256]{0:T(256)S(1)}, f32[256]{0:T(256)S(1)}, u32[]{:S(2)}, u32[]{:S(2)}) %collective-permute-start.5) | collective-permute-done | bytes 1056 | tf_op jit(solution)/shard_map/ppermute | solution.py:12
  125.7 4.8 %collective-permute-done.7 = f32[256]{0:T(256)S(1)} collective-permute-done((f32[256]{0:T(256)S(1)}, f32[256]{0:T(256)S(1)}, u32[]{:S(2)}, u32[]{:S(2)}) %collective-permute-start.7) | collective-permute-done | bytes 1056 | tf_op jit(solution)/shard_map/ppermute | solution.py:12
  130.5 4.8 %collective-permute-done.9 = f32[256]{0:T(256)S(1)} collective-permute-done((f32[256]{0:T(256)S(1)}, f32[256]{0:T(256)S(1)}, u32[]{:S(2)}, u32[]{:S(2)}) %collective-permute-start.9) | collective-permute-done | bytes 1056 | tf_op jit(solution)/shard_map/ppermute | solution.py:12
  135.6 5.2 %copy.16 = f32[4,4,256,256]{3,2,1,0:T(8,128)} copy(f32[4,4,256,256]{2,0,3,1:T(4,128)} %bitcast.11) | data formatting | bytes 8388608 | tf_op jit(solution)/shard_map/all_to_all | solution.py:39
  140.8 225.5 %while.10 = (s32[]{:T(128)}, f32[4,1024,256]{2,0,1:T(4,128)}, f32[4,1024,256]{2,1,0:T(8,128)}, f32[256,1024]{1,0:T(8,128)S(1)}, f32[256]{0:T(256)S(1)}, /*index=...) while((s32[]{:T(128)}, f32[4,1024,256]{2,0,1:T(4,128)}, ...), condition=%wide.region_3.4_spmd, body=%wide.region_2.3_spmd.sunk | while | flops 9666166784 | bytes 58733852 | solution.py:57
  141.7 4.1 fusion.100
  146.8 2.5 fusion.102
  150.4 2.5 fusion.103
  157.5 3.7 fusion.105
  163.5 3.7 fusion.106
  167.3 3.2 fusion.107
  170.5 3.6 copy.24
  174.1 23.2 %dynamic_update_slice.5 = f32[4,1024,256]{2,0,1:T(4,128)} dynamic-update-slice(f32[4,1024,256]{2,0,1:T(4,128)} %get-tuple-element.250, f32[1,1024,256]{2,0,1:T(1,128)} %copy.24, s32[]{:T(128)} %get-tuple-element.249, s32[]{:T(128)} %constant.3.clone.1..sunk, s32[]{:T(128)} %constant.3.clone.1..sunk) | dynamic-update-slice | bytes 2097156 | tf_op jit(solution)/shard_map/while/body/jit(dynamic_update_index_in_dim)/dynamic_update_slice | solution.py:57
  198.0 4.1 fusion.100
  203.2 2.5 fusion.102
  210.3 2.5 fusion.104
  213.9 3.7 fusion.105
  219.9 3.7 fusion.106
  223.6 3.2 fusion.107
  226.8 3.6 copy.24
  230.5 23.2 %dynamic_update_slice.5 = f32[4,1024,256]{2,0,1:T(4,128)} dynamic-update-slice(f32[4,1024,256]{2,0,1:T(4,128)} %get-tuple-element.250, f32[1,1024,256]{2,0,1:T(1,128)} %copy.24, s32[]{:T(128)} %get-tuple-element.249, s32[]{:T(128)} %constant.3.clone.1..sunk, s32[]{:T(128)} %constant.3.clone.1..sunk) | dynamic-update-slice | bytes 2097156 | tf_op jit(solution)/shard_map/while/body/jit(dynamic_update_index_in_dim)/dynamic_update_slice | solution.py:57
  254.4 4.1 fusion.100
  270.2 3.7 fusion.105
  276.2 3.7 fusion.106
  279.9 3.2 fusion.107
  283.2 3.6 copy.24
  286.8 23.2 %dynamic_update_slice.5 = f32[4,1024,256]{2,0,1:T(4,128)} dynamic-update-slice(f32[4,1024,256]{2,0,1:T(4,128)} %get-tuple-element.250, f32[1,1024,256]{2,0,1:T(1,128)} %copy.24, s32[]{:T(128)} %get-tuple-element.249, s32[]{:T(128)} %constant.3.clone.1..sunk, s32[]{:T(128)} %constant.3.clone.1..sunk) | dynamic-update-slice | bytes 2097156 | tf_op jit(solution)/shard_map/while/body/jit(dynamic_update_index_in_dim)/dynamic_update_slice | solution.py:57
  310.7 4.1 fusion.100
  326.5 3.7 fusion.105
  332.5 3.7 fusion.106
  336.3 3.2 fusion.107
  339.5 3.6 copy.24
  343.1 23.2 %dynamic_update_slice.5 = f32[4,1024,256]{2,0,1:T(4,128)} dynamic-update-slice(f32[4,1024,256]{2,0,1:T(4,128)} %get-tuple-element.250, f32[1,1024,256]{2,0,1:T(1,128)} %copy.24, s32[]{:T(128)} %get-tuple-element.249, s32[]{:T(128)} %constant.3.clone.1..sunk, s32[]{:T(128)} %constant.3.clone.1..sunk) | dynamic-update-slice | bytes 2097156 | tf_op jit(solution)/shard_map/while/body/jit(dynamic_update_index_in_dim)/dynamic_update_slice | solution.py:57
  366.4 48.4 %all_to_all.36 = f32[4,1024,256]{2,0,1:T(4,128)S(1)} all-to-all(f32[4,1024,256]{2,0,1:T(4,128)} %get-tuple-element.92), channel_id=1, replica_groups=mesh['blk'=8,'vb'=4] {'vb'}, dimensions={1} | all-to-all | bytes 8388608 | tf_op jit(solution)/shard_map/all_to_all | solution.py:58
  414.8 4.7 %copy.18 = f32[4,256,4,256]{3,2,1,0:T(4,128)} copy(f32[4,256,4,256]{3,0,1,2:T(4,128)S(1)} %bitcast.132) | data formatting | bytes 8388608 | tf_op jit(solution)/shard_map/all_to_all | solution.py:58
  419.5 5.8 %all_to_all.33 = f32[4,256,1024]{2,1,0:T(8,128)} reshape(f32[4,256,4,256]{3,2,1,0:T(4,128)} %copy.18) | data formatting | bytes 8388608 | tf_op jit(solution)/shard_map/all_to_all | solution.py:58
  (74 shorter events, 50.0 us)
Async XLA Ops:
  0.0 26.4 %collective-permute-start = (f32[256,1024]{1,0:T(8,128)}, f32[256,1024]{1,0:T(8,128)S(1)}, u32[]{:S(2)}, u32[]{:S(2)}) collective-permute-start(f32[256,1024]{1,0:T(8,128)} %param.9), channel_id=1, source_target_pairs={{12,0},{16,4},{20,8},{24,12},{28,16},{0,20},{4,24},{8,28},{13,1},{... | collective-permute-start | bytes 3145736 | tf_op jit(solution)/shard_map/ppermute | solution.py:12
  26.4 28.4 %collective-permute-start.2 = (f32[256,1024]{1,0:T(8,128)S(1)}, f32[256,1024]{1,0:T(8,128)S(1)}, u32[]{:S(2)}, u32[]{:S(2)}) collective-permute-start(f32[256,1024]{1,0:T(8,128)S(1)} %collective-permute-done), channel_id=1, source_target_pairs={{28,0},{0,4},{4,8},{8,12},{12,16},{16,20},{20,24},{24,28},{29,1},{... | collective-permute-start | bytes 3145736 | tf_op jit(solution)/shard_map/ppermute | solution.py:12
  54.8 16.0 %collective-permute-start.4 = (f32[256,1024]{1,0:T(8,128)S(1)}, f32[256,1024]{1,0:T(8,128)S(1)}, u32[]{:S(2)}, u32[]{:S(2)}) collective-permute-start(f32[256,1024]{1,0:T(8,128)S(1)} %collective-permute-done.2), channel_id=1, source_target_pairs={{28,0},{0,4},{4,8},{8,12},{12,16},{16,20},{20,24},{24,28},{29,1},{... | collective-permute-start | bytes 3145736 | tf_op jit(solution)/shard_map/ppermute | solution.py:12
  60.1 44.0 %copy-start.3 = (f32[1024]{0:T(1024)S(1)}, f32[1024]{0:T(1024)}, u32[]{:S(2)}) copy-start(f32[1024]{0:T(1024)} %param.13) | copy-start | bytes 12292
  60.1 44.0 %copy-start.6 = (s32[256]{0:T(256)S(1)}, s32[256]{0:T(256)}, u32[]{:S(2)}) copy-start(s32[256]{0:T(256)} %param.10) | copy-start | bytes 3076
  60.1 75.2 %copy-start.4 = (f32[256]{0:T(256)S(1)}, f32[256]{0:T(256)}, u32[]{:S(2)}) copy-start(f32[256]{0:T(256)} %param.12) | copy-start | bytes 3076
  60.1 75.2 %copy-start.5 = (s32[4,2]{0,1:T(2,128)S(1)}, s32[4,2]{0,1:T(2,128)}, u32[]{:S(2)}) copy-start(s32[4,2]{0,1:T(2,128)} %param.11) | copy-start | bytes 100
  60.1 75.5 %all-to-all-start = ((f32[4,256,1024]{1,0,2:T(4,128)}), f32[4,256,1024]{1,0,2:T(4,128)}, u32[]{:S(2)}, u32[]{:S(2)}) async-start(f32[4,256,1024]{1,0,2:T(4,128)} %copy.15), calls=%async_computation | async-start | bytes 8388608 | tf_op jit(solution)/shard_map/all_to_all | solution.py:39
  70.8 16.0 %collective-permute-start.6 = (f32[256,1024]{1,0:T(8,128)S(1)}, f32[256,1024]{1,0:T(8,128)S(1)}, u32[]{:S(2)}, u32[]{:S(2)}) collective-permute-start(f32[256,1024]{1,0:T(8,128)S(1)} %collective-permute-done.4), channel_id=1, source_target_pairs={{28,0},{0,4},{4,8},{8,12},{12,16},{16,20},{20,24},{24,28},{29,1},{... | collective-permute-start | bytes 3145736 | tf_op jit(solution)/shard_map/ppermute | solution.py:12
  86.8 1.1 copy-start.1
  87.9 16.1 %collective-permute-start.8 = (f32[256,1024]{1,0:T(8,128)S(1)}, f32[256,1024]{1,0:T(8,128)}, u32[]{:S(2)}, u32[]{:S(2)}) collective-permute-start(f32[256,1024]{1,0:T(8,128)S(1)} %collective-permute-done.6), channel_id=1, source_target_pairs={{28,0},{0,4},{4,8},{8,12},{12,16},{16,20},{20,24},{24,28},{29,1},{... | collective-permute-start | bytes 3145736 | tf_op jit(solution)/shard_map/ppermute | solution.py:12
  104.0 36.8 %collective-permute-start.10 = (f32[256,1024]{1,0:T(8,128)}, f32[256,1024]{1,0:T(8,128)}, u32[]{:S(2)}, u32[]{:S(2)}) collective-permute-start(f32[256,1024]{1,0:T(8,128)} %collective-permute-done.8), channel_id=1, source_target_pairs={{28,0},{0,4},{4,8},{8,12},{12,16},{16,20},{20,24},{24,28},{29,1},{... | collective-permute-start | bytes 3145736 | tf_op jit(solution)/shard_map/ppermute | solution.py:12
  104.3 3.1 collective-permute-start.1
  107.4 13.5 %collective-permute-start.3 = (f32[256]{0:T(256)S(1)}, f32[256]{0:T(256)S(1)}, u32[]{:S(2)}, u32[]{:S(2)}) collective-permute-start(f32[256]{0:T(256)S(1)} %collective-permute-done.1), channel_id=1, source_target_pairs={{28,0},{0,4},{4,8},{8,12},{12,16},{16,20},{20,24},{24,28},{29,1},{... | collective-permute-start | bytes 3080 | tf_op jit(solution)/shard_map/ppermute | solution.py:12
  120.9 4.8 %collective-permute-start.5 = (f32[256]{0:T(256)S(1)}, f32[256]{0:T(256)S(1)}, u32[]{:S(2)}, u32[]{:S(2)}) collective-permute-start(f32[256]{0:T(256)S(1)} %collective-permute-done.3), channel_id=1, source_target_pairs={{28,0},{0,4},{4,8},{8,12},{12,16},{16,20},{20,24},{24,28},{29,1},{... | collective-permute-start | bytes 3080 | tf_op jit(solution)/shard_map/ppermute | solution.py:12
  125.7 4.8 %collective-permute-start.7 = (f32[256]{0:T(256)S(1)}, f32[256]{0:T(256)S(1)}, u32[]{:S(2)}, u32[]{:S(2)}) collective-permute-start(f32[256]{0:T(256)S(1)} %collective-permute-done.5), channel_id=1, source_target_pairs={{28,0},{0,4},{4,8},{8,12},{12,16},{16,20},{20,24},{24,28},{29,1},{... | collective-permute-start | bytes 3080 | tf_op jit(solution)/shard_map/ppermute | solution.py:12
  130.5 4.8 %collective-permute-start.9 = (f32[256]{0:T(256)S(1)}, f32[256]{0:T(256)S(1)}, u32[]{:S(2)}, u32[]{:S(2)}) collective-permute-start(f32[256]{0:T(256)S(1)} %collective-permute-done.7), channel_id=1, source_target_pairs={{28,0},{0,4},{4,8},{8,12},{12,16},{16,20},{20,24},{24,28},{29,1},{... | collective-permute-start | bytes 3080 | tf_op jit(solution)/shard_map/ppermute | solution.py:12
  135.3 5.5 %collective-permute-start.11 = (f32[256]{0:T(256)S(1)}, f32[256]{0:T(256)S(1)}, u32[]{:S(2)}, u32[]{:S(2)}) collective-permute-start(f32[256]{0:T(256)S(1)} %collective-permute-done.9), channel_id=1, source_target_pairs={{28,0},{0,4},{4,8},{8,12},{12,16},{16,20},{20,24},{24,28},{29,1},{... | collective-permute-start | bytes 3080 | tf_op jit(solution)/shard_map/ppermute | solution.py:12
  141.0 5.8 %copy-start = (f32[4,1024,256]{2,1,0:T(8,128)S(1)}, f32[4,1024,256]{2,1,0:T(8,128)}, u32[]{:S(2)}) copy-start(f32[4,1024,256]{2,1,0:T(8,128)} %get-tuple-element.270) | copy-start | bytes 12582916 | tf_op jit(solution)/shard_map/while
  149.3 4.6 %copy-start.2 = (f32[256,1024]{1,0:T(8,128)S(1)}, f32[256,1024]{1,0:T(8,128)}, u32[]{:S(2)}) copy-start(f32[256,1024]{1,0:T(8,128)} %get-tuple-element.279) | copy-start | bytes 3145732 | tf_op jit(solution)/shard_map/while
  197.4 5.8 %copy-start = (f32[4,1024,256]{2,1,0:T(8,128)S(1)}, f32[4,1024,256]{2,1,0:T(8,128)}, u32[]{:S(2)}) copy-start(f32[4,1024,256]{2,1,0:T(8,128)} %get-tuple-element.270) | copy-start | bytes 12582916 | tf_op jit(solution)/shard_map/while
  205.7 4.6 %copy-start.2 = (f32[256,1024]{1,0:T(8,128)S(1)}, f32[256,1024]{1,0:T(8,128)}, u32[]{:S(2)}) copy-start(f32[256,1024]{1,0:T(8,128)} %get-tuple-element.279) | copy-start | bytes 3145732 | tf_op jit(solution)/shard_map/while
  253.7 5.8 %copy-start = (f32[4,1024,256]{2,1,0:T(8,128)S(1)}, f32[4,1024,256]{2,1,0:T(8,128)}, u32[]{:S(2)}) copy-start(f32[4,1024,256]{2,1,0:T(8,128)} %get-tuple-element.270) | copy-start | bytes 12582916 | tf_op jit(solution)/shard_map/while
  262.0 4.6 %copy-start.2 = (f32[256,1024]{1,0:T(8,128)S(1)}, f32[256,1024]{1,0:T(8,128)}, u32[]{:S(2)}) copy-start(f32[256,1024]{1,0:T(8,128)} %get-tuple-element.279) | copy-start | bytes 3145732 | tf_op jit(solution)/shard_map/while
  310.1 5.8 %copy-start = (f32[4,1024,256]{2,1,0:T(8,128)S(1)}, f32[4,1024,256]{2,1,0:T(8,128)}, u32[]{:S(2)}) copy-start(f32[4,1024,256]{2,1,0:T(8,128)} %get-tuple-element.270) | copy-start | bytes 12582916 | tf_op jit(solution)/shard_map/while
  318.4 4.6 %copy-start.2 = (f32[256,1024]{1,0:T(8,128)S(1)}, f32[256,1024]{1,0:T(8,128)}, u32[]{:S(2)}) copy-start(f32[256,1024]{1,0:T(8,128)} %get-tuple-element.279) | copy-start | bytes 3145732 | tf_op jit(solution)/shard_map/while
where the time goes:
time: 429 us; the launch traced here: 425 us
  local copies, waits for them, and re-layouts  132 us (31%)
  matrix products  115 us (27%)
  waiting for transfers between devices  104 us (24%)
  blocking collectives  48.4 us (11%)
  starting transfers between devices  24.3 us (6%)
    dynamic_update_slice x8, local copies, waits for them, and re-layouts, local(): totals = lax.map(pair_columns, (factors, pair_energy))  107 us
    ppermute x12, waiting for transfers between devices, passed_along(): return lax.ppermute(block, axis, route)  104 us
    dot_general x24, matrix products, pair_columns(): jnp.dot(block, factor, precision=lax.Precision.HIGHEST, preferred_element...  76.2 us
    all_to_all x1, blocking collectives, local(): return lax.all_to_all(totals, 'vb', split_axis=1, concat_axis=2, tiled=True)  48.4 us
    dot_general x24, matrix products, pair_columns(): jnp.dot(block.T, weighted / denom, precision=lax.Precision.HIGHEST, prefe...  38.5 us
    ppermute x12, starting transfers between devices, passed_along(): return lax.ppermute(block, axis, route)  19.3 us
    all_to_all x2, local copies, waits for them, and re-layouts, local(): return lax.all_to_all(totals, 'vb', split_axis=1, concat_axis=2, tiled=True)  10.4 us
  transfers between devices with their start and end apart: 13, of which 10 were waited for; matrix products, arithmetic and copies ran while one was open for 3% of the time, Pallas kernels for 0%

commit v1 on v0

--- a/solution.py
+++ b/solution.py
@@ -55,7 +55,10 @@
         return total
 
     totals = lax.map(pair_columns, (factors, pair_energy))
-    return lax.all_to_all(totals, "vb", split_axis=1, concat_axis=2, tiled=True)
+    return jnp.concatenate(
+        lax.all_to_all(jnp.stack(jnp.split(totals, lax.axis_size("vb"), axis=1)), "vb", 0, 0),
+        axis=2,
+    )
 
 
 def solution(mesh):

time: 429 us -> 321 us (0.75)
  local copies, waits for them, and re-layouts: 132 us -> 27.8 us
    dynamic_update_slice x8 -> x0, local copies, waits for them, and re-layouts: 107 us -> none  [local(): totals = lax.map(pair_columns, (factors, pair_energy))]
    reshape x0 -> x2, local copies, waits for them, and re-layouts: none -> 11.1 us  [local(): jnp.concatenate(lax.all_to_all(jnp.stack(jnp.split(totals, lax.axis_size(...]
    all_to_all x2 -> x0, local copies, waits for them, and re-layouts: 10.4 us -> none  [local(): return lax.all_to_all(totals, 'vb', split_axis=1, concat_axis=2, tiled=True)]
where the time goes in v1:
time: 321 us; the launch traced here: 319 us
  matrix products  113 us (35%)
  waiting for transfers between devices  104 us (32%)
  blocking collectives  48.1 us (15%)
  local copies, waits for them, and re-layouts  27.8 us (9%)
  starting transfers between devices  24.3 us (8%)
    ppermute x12, waiting for transfers between devices, passed_along(): return lax.ppermute(block, axis, route)  104 us
    dot_general x24, matrix products, pair_columns(): jnp.dot(block, factor, precision=lax.Precision.HIGHEST, preferred_element...  74.7 us
    all_to_all x1, blocking collectives, local(): lax.all_to_all(jnp.stack(jnp.split(totals, lax.axis_size('vb'), axis=1)),...  48.1 us
    dot_general x24, matrix products, pair_columns(): jnp.dot(block.T, weighted / denom, precision=lax.Precision.HIGHEST, prefe...  38.5 us
    ppermute x12, starting transfers between devices, passed_along(): return lax.ppermute(block, axis, route)  19.3 us
    reshape x2, local copies, waits for them, and re-layouts, local(): jnp.concatenate(lax.all_to_all(jnp.stack(jnp.split(totals, lax.axis_size(...  11.1 us
  transfers between devices with their start and end apart: 13, of which 10 were waited for; matrix products, arithmetic and copies ran while one was open for 3% of the time, Pallas kernels for 0%

profile of v1, /device:TPU:0, one launch (start us, length us, event | category | flops | bytes accessed | tf_op | source)
XLA Modules:
  0.0 319.3 jit_solution(16279006392219111150)
XLA Ops:
  0.0 3.5 %collective-permute-start = (f32[256,1024]{1,0:T(8,128)}, f32[256,1024]{1,0:T(8,128)S(1)}, u32[]{:S(2)}, u32[]{:S(2)}) collective-permute-start(f32[256,1024]{1,0:T(8,128)} %param.9), channel_id=1, source_target_pairs={{12,0},{16,4},{20,8},{24,12},{28,16},{0,20},{4,24},{8,28},{13,1},{... | collective-permute-start | bytes 3145736 | tf_op jit(solution)/shard_map/ppermute | solution.py:12
  3.5 22.9 %collective-permute-done = f32[256,1024]{1,0:T(8,128)S(1)} collective-permute-done((f32[256,1024]{1,0:T(8,128)}, f32[256,1024]{1,0:T(8,128)S(1)}, u32[]{:S(2)}, u32[]{:S(2)}) %collective-permute-start) | collective-permute-done | bytes 1048608 | tf_op jit(solution)/shard_map/ppermute | solution.py:12
  26.4 12.8 %collective-permute-start.2 = (f32[256,1024]{1,0:T(8,128)S(1)}, f32[256,1024]{1,0:T(8,128)S(1)}, u32[]{:S(2)}, u32[]{:S(2)}) collective-permute-start(f32[256,1024]{1,0:T(8,128)S(1)} %collective-permute-done), channel_id=1, source_target_pairs={{28,0},{0,4},{4,8},{8,12},{12,16},{16,20},{20,24},{24,28},{29,1},{... | collective-permute-start | bytes 3145736 | tf_op jit(solution)/shard_map/ppermute | solution.py:12
  39.2 15.6 %collective-permute-done.2 = f32[256,1024]{1,0:T(8,128)S(1)} collective-permute-done((f32[256,1024]{1,0:T(8,128)S(1)}, f32[256,1024]{1,0:T(8,128)S(1)}, u32[]{:S(2)}, u32[]{:S(2)}) %collective-permute-start.2) | collective-permute-done | bytes 1048608 | tf_op jit(solution)/shard_map/ppermute | solution.py:12
  54.8 5.3 %copy.14 = f32[4,256,1024]{1,0,2:T(4,128)} copy(f32[4,256,1024]{2,1,0:T(8,128)} %param.8) | data formatting | bytes 8388608 | tf_op args[0]
  60.1 5.0 %all-to-all-start = ((f32[4,256,1024]{1,0,2:T(4,128)}), f32[4,256,1024]{1,0,2:T(4,128)}, u32[]{:S(2)}, u32[]{:S(2)}) async-start(f32[4,256,1024]{1,0,2:T(4,128)} %copy.14), calls=%async_computation | async-start | bytes 8388608 | tf_op jit(solution)/shard_map/all_to_all | solution.py:39
  65.1 5.7 %collective-permute-done.4 = f32[256,1024]{1,0:T(8,128)S(1)} collective-permute-done((f32[256,1024]{1,0:T(8,128)S(1)}, f32[256,1024]{1,0:T(8,128)S(1)}, u32[]{:S(2)}, u32[]{:S(2)}) %collective-permute-start.4) | collective-permute-done | bytes 1048608 | tf_op jit(solution)/shard_map/ppermute | solution.py:12
  70.8 16.0 %collective-permute-done.6 = f32[256,1024]{1,0:T(8,128)S(1)} collective-permute-done((f32[256,1024]{1,0:T(8,128)S(1)}, f32[256,1024]{1,0:T(8,128)S(1)}, u32[]{:S(2)}, u32[]{:S(2)}) %collective-permute-start.6) | collective-permute-done | bytes 1048608 | tf_op jit(solution)/shard_map/ppermute | solution.py:12
  87.9 16.1 %collective-permute-done.8 = f32[256,1024]{1,0:T(8,128)} collective-permute-done((f32[256,1024]{1,0:T(8,128)S(1)}, f32[256,1024]{1,0:T(8,128)}, u32[]{:S(2)}, u32[]{:S(2)}) %collective-permute-start.8) | collective-permute-done | bytes 1048608 | tf_op jit(solution)/shard_map/ppermute | solution.py:12
  104.4 3.0 collective-permute-done.1
  107.3 3.0 collective-permute-start.3
  110.3 10.6 %collective-permute-done.3 = f32[256]{0:T(256)S(1)} collective-permute-done((f32[256]{0:T(256)S(1)}, f32[256]{0:T(256)S(1)}, u32[]{:S(2)}, u32[]{:S(2)}) %collective-permute-start.3) | collective-permute-done | bytes 1056 | tf_op jit(solution)/shard_map/ppermute | solution.py:12
  120.9 4.8 %collective-permute-done.5 = f32[256]{0:T(256)S(1)} collective-permute-done((f32[256]{0:T(256)S(1)}, f32[256]{0:T(256)S(1)}, u32[]{:S(2)}, u32[]{:S(2)}) %collective-permute-start.5) | collective-permute-done | bytes 1056 | tf_op jit(solution)/shard_map/ppermute | solution.py:12
  125.7 4.8 %collective-permute-done.7 = f32[256]{0:T(256)S(1)} collective-permute-done((f32[256]{0:T(256)S(1)}, f32[256]{0:T(256)S(1)}, u32[]{:S(2)}, u32[]{:S(2)}) %collective-permute-start.7) | collective-permute-done | bytes 1056 | tf_op jit(solution)/shard_map/ppermute | solution.py:12
  130.5 4.8 %collective-permute-done.9 = f32[256]{0:T(256)S(1)} collective-permute-done((f32[256]{0:T(256)S(1)}, f32[256]{0:T(256)S(1)}, u32[]{:S(2)}, u32[]{:S(2)}) %collective-permute-start.9) | collective-permute-done | bytes 1056 | tf_op jit(solution)/shard_map/ppermute | solution.py:12
  135.6 5.2 %copy.15 = f32[4,4,256,256]{3,2,1,0:T(8,128)} copy(f32[4,4,256,256]{2,0,3,1:T(4,128)} %bitcast.11) | data formatting | bytes 8388608 | tf_op jit(solution)/shard_map/all_to_all | solution.py:39
  140.8 116.3 %while.10 = (s32[]{:T(128)}, f32[4,1024,256]{1,2,0:T(8,128)}, f32[4,1024,256]{2,1,0:T(8,128)}, f32[256,1024]{1,0:T(8,128)S(1)}, f32[256]{0:T(256)S(1)}, /*index=...) while((s32[]{:T(128)}, f32[4,1024,256]{1,2,0:T(8,128)}, ...), condition=%wide.region_3.4_spmd, body=%wide.region_2.3_spmd.sunk | while | flops 9666166784 | bytes 54540048 | solution.py:57
  141.6 4.0 %fusion.101 = f32[256,256]{0,1:T(8,128)S(1)} fusion(f32[256,1024]{1,0:T(8,128)S(1)} %get-tuple-element.273, f32[4,1024,256]{2,1,0:T(8,128)} %get-tuple-element.272, s32[]{:T(128)} %get-tuple-element.252, f32[]{:T(128)} %bitcast.138, f32[256]{0:T(256)S(1)} %get-tuple-element.275, f32[256]{0:T(256)S(1)} %get-tuple-element.274), kind=kOutput, calls=%fused_computation.18.clone.1 | convolution fusion | flops 805502976 | bytes 2362368 | tf_op jit(solution)/shard_map/while/body/eval_jaxpr/dot_general | solution.py:46
  146.7 2.4 fusion.103
  150.2 2.5 fusion.104
  153.7 2.5 fusion.105
  157.2 3.7 %fusion.106 = f32[256,256]{0,1:T(8,128)S(1)} fusion(f32[256,1024]{1,0:T(8,128)} %get-tuple-element.283, f32[4,1024,256]{2,1,0:T(8,128)S(1)} %copy-done, s32[]{:T(128)} %get-tuple-element.252, f32[256]{0:T(256)S(1)} %get-tuple-element.284, f32[]{:T(128)} %bitcast.138, f32[256]{0:T(256)S(1)} %get-tuple-element.275), kind=kOutput, calls=%fused_computation.10.clone.1 | convolution fusion | flops 805502976 | bytes 2361352 | tf_op jit(solution)/shard_map/while/body/eval_jaxpr/dot_general | solution.py:46
  163.1 3.7 %fusion.107 = f32[256,256]{0,1:T(8,128)S(1)} fusion(f32[256,1024]{1,0:T(8,128)} %get-tuple-element.285, f32[4,1024,256]{2,1,0:T(8,128)S(1)} %copy-done, s32[]{:T(128)} %get-tuple-element.252, f32[256]{0:T(256)S(1)} %get-tuple-element.286, f32[]{:T(128)} %bitcast.138, f32[256]{0:T(256)S(1)} %get-tuple-element.275), kind=kOutput, calls=%fused_computation.8.clone.1 | convolution fusion | flops 805502976 | bytes 2361352 | tf_op jit(solution)/shard_map/while/body/eval_jaxpr/dot_general | solution.py:46
  166.8 3.2 %fusion.108 = f32[4,1024,256]{1,2,0:T(8,128)} fusion(f32[4,1024,256]{1,2,0:T(8,128)} %get-tuple-element.253, s32[]{:T(128)} %get-tuple-element.252, f32[256,1024]{1,0:T(8,128)S(1)} %convolution_add_fusion.12, f32[256,256]{0,1:T(8,128)S(1)} %fusion.107, f32[256,1024]{1,0:T(8,128)} %get-tuple-element.285), kind=kOutput, calls=%fused_computation.2.clone.1 | convolution fusion | flops 805568512 | bytes 3408384 | tf_op jit(solution)/shard_map/while/body/eval_jaxpr/dot_general | solution.py:49
  170.7 4.0 %fusion.101 = f32[256,256]{0,1:T(8,128)S(1)} fusion(f32[256,1024]{1,0:T(8,128)S(1)} %get-tuple-element.273, f32[4,1024,256]{2,1,0:T(8,128)} %get-tuple-element.272, s32[]{:T(128)} %get-tuple-element.252, f32[]{:T(128)} %bitcast.138, f32[256]{0:T(256)S(1)} %get-tuple-element.275, f32[256]{0:T(256)S(1)} %get-tuple-element.274), kind=kOutput, calls=%fused_computation.18.clone.1 | convolution fusion | flops 805502976 | bytes 2362368 | tf_op jit(solution)/shard_map/while/body/eval_jaxpr/dot_general | solution.py:46
  175.7 2.4 fusion.103
  179.2 2.5 fusion.104
  182.7 2.5 fusion.105
  186.2 3.7 %fusion.106 = f32[256,256]{0,1:T(8,128)S(1)} fusion(f32[256,1024]{1,0:T(8,128)} %get-tuple-element.283, f32[4,1024,256]{2,1,0:T(8,128)S(1)} %copy-done, s32[]{:T(128)} %get-tuple-element.252, f32[256]{0:T(256)S(1)} %get-tuple-element.284, f32[]{:T(128)} %bitcast.138, f32[256]{0:T(256)S(1)} %get-tuple-element.275), kind=kOutput, calls=%fused_computation.10.clone.1 | convolution fusion | flops 805502976 | bytes 2361352 | tf_op jit(solution)/shard_map/while/body/eval_jaxpr/dot_general | solution.py:46
  192.2 3.7 %fusion.107 = f32[256,256]{0,1:T(8,128)S(1)} fusion(f32[256,1024]{1,0:T(8,128)} %get-tuple-element.285, f32[4,1024,256]{2,1,0:T(8,128)S(1)} %copy-done, s32[]{:T(128)} %get-tuple-element.252, f32[256]{0:T(256)S(1)} %get-tuple-element.286, f32[]{:T(128)} %bitcast.138, f32[256]{0:T(256)S(1)} %get-tuple-element.275), kind=kOutput, calls=%fused_computation.8.clone.1 | convolution fusion | flops 805502976 | bytes 2361352 | tf_op jit(solution)/shard_map/while/body/eval_jaxpr/dot_general | solution.py:46
  195.8 3.2 %fusion.108 = f32[4,1024,256]{1,2,0:T(8,128)} fusion(f32[4,1024,256]{1,2,0:T(8,128)} %get-tuple-element.253, s32[]{:T(128)} %get-tuple-element.252, f32[256,1024]{1,0:T(8,128)S(1)} %convolution_add_fusion.12, f32[256,256]{0,1:T(8,128)S(1)} %fusion.107, f32[256,1024]{1,0:T(8,128)} %get-tuple-element.285), kind=kOutput, calls=%fused_computation.2.clone.1 | convolution fusion | flops 805568512 | bytes 3408384 | tf_op jit(solution)/shard_map/while/body/eval_jaxpr/dot_general | solution.py:49
  199.7 4.0 %fusion.101 = f32[256,256]{0,1:T(8,128)S(1)} fusion(f32[256,1024]{1,0:T(8,128)S(1)} %get-tuple-element.273, f32[4,1024,256]{2,1,0:T(8,128)} %get-tuple-element.272, s32[]{:T(128)} %get-tuple-element.252, f32[]{:T(128)} %bitcast.138, f32[256]{0:T(256)S(1)} %get-tuple-element.275, f32[256]{0:T(256)S(1)} %get-tuple-element.274), kind=kOutput, calls=%fused_computation.18.clone.1 | convolution fusion | flops 805502976 | bytes 2362368 | tf_op jit(solution)/shard_map/while/body/eval_jaxpr/dot_general | solution.py:46
  204.7 2.4 fusion.103
  208.2 2.5 fusion.104
  211.8 2.5 fusion.105
  215.3 3.7 %fusion.106 = f32[256,256]{0,1:T(8,128)S(1)} fusion(f32[256,1024]{1,0:T(8,128)} %get-tuple-element.283, f32[4,1024,256]{2,1,0:T(8,128)S(1)} %copy-done, s32[]{:T(128)} %get-tuple-element.252, f32[256]{0:T(256)S(1)} %get-tuple-element.284, f32[]{:T(128)} %bitcast.138, f32[256]{0:T(256)S(1)} %get-tuple-element.275), kind=kOutput, calls=%fused_computation.10.clone.1 | convolution fusion | flops 805502976 | bytes 2361352 | tf_op jit(solution)/shard_map/while/body/eval_jaxpr/dot_general | solution.py:46
  221.2 3.7 %fusion.107 = f32[256,256]{0,1:T(8,128)S(1)} fusion(f32[256,1024]{1,0:T(8,128)} %get-tuple-element.285, f32[4,1024,256]{2,1,0:T(8,128)S(1)} %copy-done, s32[]{:T(128)} %get-tuple-element.252, f32[256]{0:T(256)S(1)} %get-tuple-element.286, f32[]{:T(128)} %bitcast.138, f32[256]{0:T(256)S(1)} %get-tuple-element.275), kind=kOutput, calls=%fused_computation.8.clone.1 | convolution fusion | flops 805502976 | bytes 2361352 | tf_op jit(solution)/shard_map/while/body/eval_jaxpr/dot_general | solution.py:46
  224.9 3.2 %fusion.108 = f32[4,1024,256]{1,2,0:T(8,128)} fusion(f32[4,1024,256]{1,2,0:T(8,128)} %get-tuple-element.253, s32[]{:T(128)} %get-tuple-element.252, f32[256,1024]{1,0:T(8,128)S(1)} %convolution_add_fusion.12, f32[256,256]{0,1:T(8,128)S(1)} %fusion.107, f32[256,1024]{1,0:T(8,128)} %get-tuple-element.285), kind=kOutput, calls=%fused_computation.2.clone.1 | convolution fusion | flops 805568512 | bytes 3408384 | tf_op jit(solution)/shard_map/while/body/eval_jaxpr/dot_general | solution.py:49
  228.7 4.0 %fusion.101 = f32[256,256]{0,1:T(8,128)S(1)} fusion(f32[256,1024]{1,0:T(8,128)S(1)} %get-tuple-element.273, f32[4,1024,256]{2,1,0:T(8,128)} %get-tuple-element.272, s32[]{:T(128)} %get-tuple-element.252, f32[]{:T(128)} %bitcast.138, f32[256]{0:T(256)S(1)} %get-tuple-element.275, f32[256]{0:T(256)S(1)} %get-tuple-element.274), kind=kOutput, calls=%fused_computation.18.clone.1 | convolution fusion | flops 805502976 | bytes 2362368 | tf_op jit(solution)/shard_map/while/body/eval_jaxpr/dot_general | solution.py:46
  237.3 2.5 fusion.104
  240.8 2.5 fusion.105
  244.3 3.7 %fusion.106 = f32[256,256]{0,1:T(8,128)S(1)} fusion(f32[256,1024]{1,0:T(8,128)} %get-tuple-element.283, f32[4,1024,256]{2,1,0:T(8,128)S(1)} %copy-done, s32[]{:T(128)} %get-tuple-element.252, f32[256]{0:T(256)S(1)} %get-tuple-element.284, f32[]{:T(128)} %bitcast.138, f32[256]{0:T(256)S(1)} %get-tuple-element.275), kind=kOutput, calls=%fused_computation.10.clone.1 | convolution fusion | flops 805502976 | bytes 2361352 | tf_op jit(solution)/shard_map/while/body/eval_jaxpr/dot_general | solution.py:46
  250.2 3.7 %fusion.107 = f32[256,256]{0,1:T(8,128)S(1)} fusion(f32[256,1024]{1,0:T(8,128)} %get-tuple-element.285, f32[4,1024,256]{2,1,0:T(8,128)S(1)} %copy-done, s32[]{:T(128)} %get-tuple-element.252, f32[256]{0:T(256)S(1)} %get-tuple-element.286, f32[]{:T(128)} %bitcast.138, f32[256]{0:T(256)S(1)} %get-tuple-element.275), kind=kOutput, calls=%fused_computation.8.clone.1 | convolution fusion | flops 805502976 | bytes 2361352 | tf_op jit(solution)/shard_map/while/body/eval_jaxpr/dot_general | solution.py:46
  253.9 3.2 %fusion.108 = f32[4,1024,256]{1,2,0:T(8,128)} fusion(f32[4,1024,256]{1,2,0:T(8,128)} %get-tuple-element.253, s32[]{:T(128)} %get-tuple-element.252, f32[256,1024]{1,0:T(8,128)S(1)} %convolution_add_fusion.12, f32[256,256]{0,1:T(8,128)S(1)} %fusion.107, f32[256,1024]{1,0:T(8,128)} %get-tuple-element.285), kind=kOutput, calls=%fused_computation.2.clone.1 | convolution fusion | flops 805568512 | bytes 3408384 | tf_op jit(solution)/shard_map/while/body/eval_jaxpr/dot_general | solution.py:49
  257.1 2.6 slice_bitcast_fusion.3
  260.2 48.1 %all_to_all.23 = f32[4,4,256,256]{2,3,1,0:T(8,128)} all-to-all(f32[4,4,256,256]{2,3,1,0:T(8,128)S(1)} %pad_maximum_fusion), channel_id=1, replica_groups=mesh['blk'=8,'vb'=4] {'vb'}, dimensions={0} | all-to-all | bytes 8388608 | tf_op jit(solution)/shard_map/all_to_all | solution.py:59
  308.2 5.3 %copy.16 = f32[4,256,4,256]{3,2,1,0:T(4,128)} copy(f32[4,256,4,256]{1,3,0,2:T(8,128)} %bitcast.140) | data formatting | bytes 8388608 | tf_op jit(solution)/shard_map/reshape | solution.py:58
  313.5 5.8 %reshape.18 = f32[4,256,1024]{2,1,0:T(8,128)} reshape(f32[4,256,4,256]{3,2,1,0:T(4,128)} %copy.16) | data formatting | bytes 8388608 | tf_op jit(solution)/shard_map/reshape | solution.py:58
  (68 shorter events, 32.6 us)
Async XLA Ops:
  0.0 26.4 %collective-permute-start = (f32[256,1024]{1,0:T(8,128)}, f32[256,1024]{1,0:T(8,128)S(1)}, u32[]{:S(2)}, u32[]{:S(2)}) collective-permute-start(f32[256,1024]{1,0:T(8,128)} %param.9), channel_id=1, source_target_pairs={{12,0},{16,4},{20,8},{24,12},{28,16},{0,20},{4,24},{8,28},{13,1},{... | collective-permute-start | bytes 3145736 | tf_op jit(solution)/shard_map/ppermute | solution.py:12
  26.4 28.4 %collective-permute-start.2 = (f32[256,1024]{1,0:T(8,128)S(1)}, f32[256,1024]{1,0:T(8,128)S(1)}, u32[]{:S(2)}, u32[]{:S(2)}) collective-permute-start(f32[256,1024]{1,0:T(8,128)S(1)} %collective-permute-done), channel_id=1, source_target_pairs={{28,0},{0,4},{4,8},{8,12},{12,16},{16,20},{20,24},{24,28},{29,1},{... | collective-permute-start | bytes 3145736 | tf_op jit(solution)/shard_map/ppermute | solution.py:12
  54.8 16.0 %collective-permute-start.4 = (f32[256,1024]{1,0:T(8,128)S(1)}, f32[256,1024]{1,0:T(8,128)S(1)}, u32[]{:S(2)}, u32[]{:S(2)}) collective-permute-start(f32[256,1024]{1,0:T(8,128)S(1)} %collective-permute-done.2), channel_id=1, source_target_pairs={{28,0},{0,4},{4,8},{8,12},{12,16},{16,20},{20,24},{24,28},{29,1},{... | collective-permute-start | bytes 3145736 | tf_op jit(solution)/shard_map/ppermute | solution.py:12
  60.1 44.0 %copy-start.3 = (f32[1024]{0:T(1024)S(1)}, f32[1024]{0:T(1024)}, u32[]{:S(2)}) copy-start(f32[1024]{0:T(1024)} %param.13) | copy-start | bytes 12292
  60.1 44.0 %copy-start.6 = (s32[256]{0:T(256)S(1)}, s32[256]{0:T(256)}, u32[]{:S(2)}) copy-start(s32[256]{0:T(256)} %param.10) | copy-start | bytes 3076
  60.1 75.2 %copy-start.4 = (f32[256]{0:T(256)S(1)}, f32[256]{0:T(256)}, u32[]{:S(2)}) copy-start(f32[256]{0:T(256)} %param.12) | copy-start | bytes 3076
  60.1 75.2 %copy-start.5 = (s32[4,2]{0,1:T(2,128)S(1)}, s32[4,2]{0,1:T(2,128)}, u32[]{:S(2)}) copy-start(s32[4,2]{0,1:T(2,128)} %param.11) | copy-start | bytes 100
  60.1 75.5 %all-to-all-start = ((f32[4,256,1024]{1,0,2:T(4,128)}), f32[4,256,1024]{1,0,2:T(4,128)}, u32[]{:S(2)}, u32[]{:S(2)}) async-start(f32[4,256,1024]{1,0,2:T(4,128)} %copy.14), calls=%async_computation | async-start | bytes 8388608 | tf_op jit(solution)/shard_map/all_to_all | solution.py:39
  70.8 16.0 %collective-permute-start.6 = (f32[256,1024]{1,0:T(8,128)S(1)}, f32[256,1024]{1,0:T(8,128)S(1)}, u32[]{:S(2)}, u32[]{:S(2)}) collective-permute-start(f32[256,1024]{1,0:T(8,128)S(1)} %collective-permute-done.4), channel_id=1, source_target_pairs={{28,0},{0,4},{4,8},{8,12},{12,16},{16,20},{20,24},{24,28},{29,1},{... | collective-permute-start | bytes 3145736 | tf_op jit(solution)/shard_map/ppermute | solution.py:12
  86.8 1.1 copy-start.1
  87.9 16.1 %collective-permute-start.8 = (f32[256,1024]{1,0:T(8,128)S(1)}, f32[256,1024]{1,0:T(8,128)}, u32[]{:S(2)}, u32[]{:S(2)}) collective-permute-start(f32[256,1024]{1,0:T(8,128)S(1)} %collective-permute-done.6), channel_id=1, source_target_pairs={{28,0},{0,4},{4,8},{8,12},{12,16},{16,20},{20,24},{24,28},{29,1},{... | collective-permute-start | bytes 3145736 | tf_op jit(solution)/shard_map/ppermute | solution.py:12
  104.0 36.8 %collective-permute-start.10 = (f32[256,1024]{1,0:T(8,128)}, f32[256,1024]{1,0:T(8,128)}, u32[]{:S(2)}, u32[]{:S(2)}) collective-permute-start(f32[256,1024]{1,0:T(8,128)} %collective-permute-done.8), channel_id=1, source_target_pairs={{28,0},{0,4},{4,8},{8,12},{12,16},{16,20},{20,24},{24,28},{29,1},{... | collective-permute-start | bytes 3145736 | tf_op jit(solution)/shard_map/ppermute | solution.py:12
  104.3 3.1 collective-permute-start.1
  107.3 13.5 %collective-permute-start.3 = (f32[256]{0:T(256)S(1)}, f32[256]{0:T(256)S(1)}, u32[]{:S(2)}, u32[]{:S(2)}) collective-permute-start(f32[256]{0:T(256)S(1)} %collective-permute-done.1), channel_id=1, source_target_pairs={{28,0},{0,4},{4,8},{8,12},{12,16},{16,20},{20,24},{24,28},{29,1},{... | collective-permute-start | bytes 3080 | tf_op jit(solution)/shard_map/ppermute | solution.py:12
  120.9 4.8 %collective-permute-start.5 = (f32[256]{0:T(256)S(1)}, f32[256]{0:T(256)S(1)}, u32[]{:S(2)}, u32[]{:S(2)}) collective-permute-start(f32[256]{0:T(256)S(1)} %collective-permute-done.3), channel_id=1, source_target_pairs={{28,0},{0,4},{4,8},{8,12},{12,16},{16,20},{20,24},{24,28},{29,1},{... | collective-permute-start | bytes 3080 | tf_op jit(solution)/shard_map/ppermute | solution.py:12
  125.7 4.8 %collective-permute-start.7 = (f32[256]{0:T(256)S(1)}, f32[256]{0:T(256)S(1)}, u32[]{:S(2)}, u32[]{:S(2)}) collective-permute-start(f32[256]{0:T(256)S(1)} %collective-permute-done.5), channel_id=1, source_target_pairs={{28,0},{0,4},{4,8},{8,12},{12,16},{16,20},{20,24},{24,28},{29,1},{... | collective-permute-start | bytes 3080 | tf_op jit(solution)/shard_map/ppermute | solution.py:12
  130.5 4.8 %collective-permute-start.9 = (f32[256]{0:T(256)S(1)}, f32[256]{0:T(256)S(1)}, u32[]{:S(2)}, u32[]{:S(2)}) collective-permute-start(f32[256]{0:T(256)S(1)} %collective-permute-done.7), channel_id=1, source_target_pairs={{28,0},{0,4},{4,8},{8,12},{12,16},{16,20},{20,24},{24,28},{29,1},{... | collective-permute-start | bytes 3080 | tf_op jit(solution)/shard_map/ppermute | solution.py:12
  135.3 5.5 %collective-permute-start.11 = (f32[256]{0:T(256)S(1)}, f32[256]{0:T(256)S(1)}, u32[]{:S(2)}, u32[]{:S(2)}) collective-permute-start(f32[256]{0:T(256)S(1)} %collective-permute-done.9), channel_id=1, source_target_pairs={{28,0},{0,4},{4,8},{8,12},{12,16},{16,20},{20,24},{24,28},{29,1},{... | collective-permute-start | bytes 3080 | tf_op jit(solution)/shard_map/ppermute | solution.py:12
  141.0 5.7 %copy-start = (f32[4,1024,256]{2,1,0:T(8,128)S(1)}, f32[4,1024,256]{2,1,0:T(8,128)}, u32[]{:S(2)}) copy-start(f32[4,1024,256]{2,1,0:T(8,128)} %get-tuple-element.272) | copy-start | bytes 12582916 | tf_op jit(solution)/shard_map/while
  149.1 4.6 %copy-start.2 = (f32[256,1024]{1,0:T(8,128)S(1)}, f32[256,1024]{1,0:T(8,128)}, u32[]{:S(2)}) copy-start(f32[256,1024]{1,0:T(8,128)} %get-tuple-element.281) | copy-start | bytes 3145732 | tf_op jit(solution)/shard_map/while
  170.1 5.6 %copy-start = (f32[4,1024,256]{2,1,0:T(8,128)S(1)}, f32[4,1024,256]{2,1,0:T(8,128)}, u32[]{:S(2)}) copy-start(f32[4,1024,256]{2,1,0:T(8,128)} %get-tuple-element.272) | copy-start | bytes 12582916 | tf_op jit(solution)/shard_map/while
  178.2 4.6 %copy-start.2 = (f32[256,1024]{1,0:T(8,128)S(1)}, f32[256,1024]{1,0:T(8,128)}, u32[]{:S(2)}) copy-start(f32[256,1024]{1,0:T(8,128)} %get-tuple-element.281) | copy-start | bytes 3145732 | tf_op jit(solution)/shard_map/while
  199.1 5.6 %copy-start = (f32[4,1024,256]{2,1,0:T(8,128)S(1)}, f32[4,1024,256]{2,1,0:T(8,128)}, u32[]{:S(2)}) copy-start(f32[4,1024,256]{2,1,0:T(8,128)} %get-tuple-element.272) | copy-start | bytes 12582916 | tf_op jit(solution)/shard_map/while
  207.2 4.6 %copy-start.2 = (f32[256,1024]{1,0:T(8,128)S(1)}, f32[256,1024]{1,0:T(8,128)}, u32[]{:S(2)}) copy-start(f32[256,1024]{1,0:T(8,128)} %get-tuple-element.281) | copy-start | bytes 3145732 | tf_op jit(solution)/shard_map/while
  228.1 5.6 %copy-start = (f32[4,1024,256]{2,1,0:T(8,128)S(1)}, f32[4,1024,256]{2,1,0:T(8,128)}, u32[]{:S(2)}) copy-start(f32[4,1024,256]{2,1,0:T(8,128)} %get-tuple-element.272) | copy-start | bytes 12582916 | tf_op jit(solution)/shard_map/while
  236.2 4.6 %copy-start.2 = (f32[256,1024]{1,0:T(8,128)S(1)}, f32[256,1024]{1,0:T(8,128)}, u32[]{:S(2)}) copy-start(f32[256,1024]{1,0:T(8,128)} %get-tuple-element.281) | copy-start | bytes 3145732 | tf_op jit(solution)/shard_map/while
